TPU v7x, 32 devices: a whole 2x2x4 slice. The times are simulated.
32 devices in a mesh: dp: 8 (over y, x, core), expert: 4 (over z).
Axes of the slice: x: 2, y: 2, z: 4, core: 2. Of those that a mesh axis runs over, the one named last changes fastest.
Arguments:
- hidden: bfloat16 [2, 512, 2880], P(None, ('dp', 'expert')), may hold values from -1.5 to 1.5
- norm_gain: float32 [2880], replicated, may hold values from 0.1 to 1.9
- router: bfloat16 [2880, 64], replicated, may hold values from -0.078125 to 0.078125
- routes: int32 [2, 512, 4], P(None, ('dp', 'expert')), may hold values from 0 to 63, all different within a row; in each aligned block of 16 rows (0 to 15, 16 to 31, ..., all dimensions but the last counted through in order) at most 2 rows name the same one
- w_gate: bfloat16 [64, 2880, 2048], P('expert', None, 'dp'), may hold values from -0.109375 to 0.109375
- w_up: bfloat16 [64, 2880, 2048], P('expert', None, 'dp'), may hold values from -0.109375 to 0.109375
- w_down: bfloat16 [64, 2048, 2880], P('expert', 'dp'), may hold values from -0.125 to 0.125
- queries: bfloat16 [2, 512, 4096], P(None, ('dp', 'expert')), may hold values from -5.5 to 5.5
- new_key: bfloat16 [2, 512, 512], P(None, ('dp', 'expert')), may hold values from -8 to 8
- new_value: bfloat16 [2, 512, 512], P(None, ('dp', 'expert')), may hold values from -6 to 6
- key_pages: bfloat16 [256, 4, 16, 512], P(('dp', 'expert')), may hold values from -6 to 6
- value_pages: bfloat16 [256, 4, 16, 512], P(('dp', 'expert')), may hold values from -6 to 6
- page_counts: int32 [32, 16], P(('dp', 'expert')), may hold values from 1 to 10, 32 in all within a row
- page_order: int32 [32, 32], P(('dp', 'expert')), may hold values from 0 to 31, each once within a row
Outputs:
- context: bfloat16 [2, 512, 4096], P(None, ('dp', 'expert'))
- layer_out: bfloat16 [2, 512, 2880], P(None, ('dp', 'expert'))
Inputs may be any that keep to these rules, and one draw needn't show every extreme that they name: `routes`: in each step, the 16 rows of one aligned block name each expert at most 2 times, and some block names some expert exactly 2 times. `page_counts`: each block's counts sum to 32, and the largest count of a block is exactly 10. Each row of page_order is a permutation of 0 to 31.
All inputs are finite; a program needn't handle non-finite values.
Results may differ from a plain program's by a relative error of at most 0.0095.
Values may be sent and summed in bfloat16 or wider, within the bound.
No kernel may reach another device: no remote copies, remote signals or barrier semaphores. Data moves between devices by JAX's collectives and lax.ppermute only.
A program may use at most 192 MiB of HBM per device.

v0:
```python
import jax
import jax.numpy as jnp
from jax import lax
from jax.sharding import PartitionSpec as P

HEADS = 64
KV_HEADS = 8
HEAD_DIM = 64
EXPERTS = 64
MOST = 2
STEPS = 2
BLOCK = 16


def page_layout(counts, page_perm, most_pages):
    starts = jnp.cumsum(counts) - counts
    offsets = jnp.arange(most_pages, dtype=jnp.int32)
    places = starts[:, None] + offsets[None, :]
    places = jnp.where(offsets[None, :] < counts[:, None], places, 0)
    return jnp.take(page_perm, places, axis=0)


def attention(query_rows, fresh_keys, fresh_values, space_keys, space_values, counts, page_perm):
    group_size = HEADS // KV_HEADS
    most_pages = page_perm.shape[0] // 3
    row_count = counts.shape[0]
    cache_span = most_pages * BLOCK
    slot_ids = page_layout(counts, page_perm, most_pages).reshape(-1)
    cache_keys = jnp.take(space_keys, slot_ids, axis=0).reshape(
        row_count, cache_span, KV_HEADS, HEAD_DIM
    )
    cache_values = jnp.take(space_values, slot_ids, axis=0).reshape(
        row_count, cache_span, KV_HEADS, HEAD_DIM
    )
    live_mask = jnp.arange(cache_span)[None, :] < (counts * BLOCK)[:, None]
    query_heads = query_rows.reshape(STEPS, row_count, KV_HEADS, group_size, HEAD_DIM)
    new_keys = fresh_keys.reshape(STEPS, row_count, KV_HEADS, HEAD_DIM)
    new_values = fresh_values.reshape(STEPS, row_count, KV_HEADS, HEAD_DIM)
    score_scale = HEAD_DIM ** (-0.5)
    old_scores = (
        jnp.einsum("trkgh,rlkh->trkgl", query_heads, cache_keys, preferred_element_type=jnp.float32)
        * score_scale
    )
    old_scores = jnp.where(live_mask[None, :, None, None, :], old_scores, -jnp.inf)
    new_scores = (
        jnp.einsum("trkgh,urkh->trkgu", query_heads, new_keys, preferred_element_type=jnp.float32)
        * score_scale
    )
    causal = jnp.arange(STEPS)[None, :] <= jnp.arange(STEPS)[:, None]
    new_scores = jnp.where(causal[:, None, None, None, :], new_scores, -jnp.inf)
    row_max = jnp.maximum(jnp.max(old_scores, axis=-1), jnp.max(new_scores, axis=-1))
    old_probs = jnp.exp(old_scores - row_max[..., None])
    new_probs = jnp.exp(new_scores - row_max[..., None])
    denominator = jnp.sum(old_probs, axis=-1) + jnp.sum(new_probs, axis=-1)
    numerator = jnp.einsum(
        "trkgl,rlkh->trkgh",
        old_probs.astype(jnp.bfloat16),
        cache_values,
        preferred_element_type=jnp.float32,
    )
    numerator = numerator + jnp.einsum(
        "trkgu,urkh->trkgh",
        new_probs.astype(jnp.bfloat16),
        new_values,
        preferred_element_type=jnp.float32,
    )
    result = numerator / denominator[..., None]
    return result.reshape(STEPS, row_count, HEADS * HEAD_DIM).astype(jnp.bfloat16)


def route_tables(expert_ids, gate_vals):
    numbers = jnp.arange(EXPERTS, dtype=jnp.int32)
    picked = (expert_ids[..., None] == numbers).astype(jnp.int32)
    per_row = jnp.sum(picked, axis=2)
    earlier = jnp.cumsum(per_row, axis=1) - per_row
    rank_vals = jnp.sum(picked * earlier[:, :, None, :], axis=3)
    targets = expert_ids * MOST + rank_vals
    places = jnp.arange(EXPERTS * MOST, dtype=jnp.int32)
    matches = targets[..., None] == places
    sender = jnp.any(matches, axis=2).astype(jnp.bfloat16)
    weights = jnp.sum(
        jnp.where(matches, gate_vals[..., None].astype(jnp.float32), 0.0), axis=2
    ).astype(jnp.bfloat16)
    return (sender, weights)


def expert_block(slot_rows, w_gate, w_up, w_down):
    gate_part = jnp.einsum(
        "pkxmd,xdf->pkxmf", slot_rows, w_gate, preferred_element_type=jnp.float32
    )
    up_part = jnp.einsum("pkxmd,xdf->pkxmf", slot_rows, w_up, preferred_element_type=jnp.float32)
    hidden_act = ((up_part + 1.0) * gate_part * jax.nn.sigmoid(1.702 * gate_part)).astype(
        jnp.bfloat16
    )
    return jnp.einsum(
        "pkxmf,xfd->pkxmd", hidden_act, w_down, preferred_element_type=jnp.float32
    ).astype(jnp.bfloat16)


def moe_step(hidden_rows, norm_gain, router, expert_ids, w_gate, w_up, w_down):
    residual = hidden_rows.astype(jnp.float32)
    scale_rows = lax.rsqrt(jnp.mean(residual * residual, axis=1, keepdims=True) + 1e-05)
    normed = (residual * scale_rows * norm_gain).astype(jnp.bfloat16)
    logit_rows = jnp.dot(normed, router, preferred_element_type=jnp.float32)
    numbers = jnp.arange(EXPERTS, dtype=jnp.int32)
    chosen = jnp.sum(
        jnp.where(expert_ids[..., None] == numbers, logit_rows[:, None, :], 0.0), axis=-1
    )
    spreads = chosen[:, None, :] - chosen[:, :, None]
    gate_vals = (1.0 / jnp.sum(jnp.exp(spreads), axis=2)).astype(jnp.bfloat16)
    model_width = residual.shape[1]
    columns = lax.axis_size("expert")
    local_experts = w_gate.shape[0]
    group_rows, group_ids, group_gates = (
        lax.all_gather(normed[None], "dp", axis=0, tiled=True),
        lax.all_gather(expert_ids.astype(jnp.bfloat16)[None], "dp", axis=0, tiled=True),
        lax.all_gather(gate_vals[None], "dp", axis=0, tiled=True),
    )
    sender, weights = route_tables(group_ids.astype(jnp.int32), group_gates)
    packed = jnp.einsum(
        "prs,prd->psd", sender, group_rows, preferred_element_type=jnp.float32
    ).astype(jnp.bfloat16)
    packed = packed.reshape(packed.shape[0], columns, local_experts, MOST, model_width)
    partial_out = expert_block(
        lax.all_to_all(packed, "expert", split_axis=1, concat_axis=1, tiled=True),
        w_gate,
        w_up,
        w_down,
    )
    returned = lax.all_to_all(partial_out, "expert", split_axis=1, concat_axis=1, tiled=True)
    returned = returned.reshape(returned.shape[0], EXPERTS * MOST, model_width)
    row_terms = jnp.einsum("prs,psd->prd", weights, returned, preferred_element_type=jnp.float32)
    branch_out = lax.psum_scatter(row_terms, "dp", scatter_dimension=0, tiled=True)[0]
    return (residual + branch_out).astype(jnp.bfloat16)


def body(
    hidden,
    norm_gain,
    router,
    routes,
    w_gate,
    w_up,
    w_down,
    queries,
    new_key,
    new_value,
    key_pages,
    value_pages,
    page_counts,
    page_order,
):
    host_keys, host_values = (
        lax.all_to_all(key_pages, "dp", split_axis=0, concat_axis=0, tiled=True),
        lax.all_to_all(value_pages, "dp", split_axis=0, concat_axis=0, tiled=True),
    )
    kv_width = KV_HEADS * HEAD_DIM
    space_keys = host_keys.reshape(-1, BLOCK, kv_width)
    space_values = host_values.reshape(-1, BLOCK, kv_width)
    context = attention(
        queries, new_key, new_value, space_keys, space_values, page_counts[0], page_order[0]
    )
    outputs = []
    for step_index in range(STEPS):
        outputs.append(
            moe_step(
                hidden[step_index], norm_gain, router, routes[step_index], w_gate, w_up, w_down
            )
        )
    return (context, jnp.stack(outputs))


def solution(mesh):
    return jax.shard_map(
        body,
        mesh=mesh,
        in_specs=(
            P(None, ("dp", "expert"), None),
            P(),
            P(),
            P(None, ("dp", "expert"), None),
            P("expert", None, "dp"),
            P("expert", None, "dp"),
            P("expert", "dp", None),
            P(None, ("dp", "expert"), None),
            P(None, ("dp", "expert"), None),
            P(None, ("dp", "expert"), None),
            P(("dp", "expert"), None, None, None),
            P(("dp", "expert"), None, None, None),
            P(("dp", "expert"), None),
            P(("dp", "expert"), None),
        ),
        out_specs=(P(None, ("dp", "expert"), None), P(None, ("dp", "expert"), None)),
        check_vma=False,
    )
```

profile of v0, /device:TPU:0, one launch (start us, length us, event | category | flops | bytes accessed | tf_op | source)
XLA Modules:
  0.0 657.7 jit_solution(8892093810396671834)
XLA Ops:
  7.2 5.3 all-to-all-start
  12.5 0.7 slice_bitcast_fusion.1
  13.2 12.1 %all_gather.18 = bf16[8,16,4]{1,2,0:T(4,128)(2,1)S(1)} all-gather(bf16[1,16,4]{1,2,0:T(4,128)(2,1)S(1)} %get-tuple-element.14), channel_id=1, replica_groups=mesh['dp'=8,'expert'=4] {'dp'}, dimensions={0}, use_global_device_ids=true | all-gather | bytes 1152 | tf_op jit(solution)/shard_map/all_gather | solution.py:116
  25.5 1.1 fusion.105
  26.6 1.1 fusion.109
  27.7 0.7 select_reduce_fusion.3
  28.4 9.4 %all_gather.20 = bf16[8,16,2880]{2,1,0:T(8,128)(2,1)S(1)} all-gather(bf16[1,16,2880]{2,1,0:T(8,128)(2,1)S(1)} %get-tuple-element.7), channel_id=1, replica_groups=mesh['dp'=8,'expert'=4] {'dp'}, dimensions={0}, use_global_device_ids=true | all-gather | bytes 829440 | tf_op jit(solution)/shard_map/all_gather | solution.py:115
  37.8 3.5 all-to-all-start.1
  41.5 4.0 convolution_convert_fusion.1
  45.5 8.8 %copy.98 = bf16[8,128,2880]{2,0,1:T(8,128)(2,1)} copy(bf16[8,128,2880]{1,2,0:T(8,128)(2,1)} %convolution_convert_fusion.1) | data formatting | bytes 11796480 | tf_op jit(solution)/shard_map/convert_element_type | solution.py:122
  54.3 5.2 all-to-all-start.2
  59.5 9.3 %all_gather.21 = bf16[8,16,4]{1,2,0:T(4,128)(2,1)S(1)} all-gather(bf16[1,16,4]{1,2,0:T(4,128)(2,1)S(1)} %get-tuple-element.13), channel_id=1, replica_groups=mesh['dp'=8,'expert'=4] {'dp'}, dimensions={0}, use_global_device_ids=true | all-gather | bytes 1152 | tf_op jit(solution)/shard_map/all_gather | solution.py:116
  69.0 0.7 select_reduce_fusion.1
  69.9 10.4 %all_gather.23 = bf16[8,16,2880]{2,1,0:T(8,128)(2,1)S(1)} all-gather(bf16[1,16,2880]{2,1,0:T(8,128)(2,1)S(1)} %get-tuple-element.8), channel_id=1, replica_groups=mesh['dp'=8,'expert'=4] {'dp'}, dimensions={0}, use_global_device_ids=true | all-gather | bytes 829440 | tf_op jit(solution)/shard_map/all_gather | solution.py:115
  80.3 4.0 convolution_convert_fusion
  84.2 8.8 %copy.106 = bf16[8,128,2880]{2,0,1:T(8,128)(2,1)} copy(bf16[8,128,2880]{1,2,0:T(8,128)(2,1)} %convolution_convert_fusion) | data formatting | bytes 11796480 | tf_op jit(solution)/shard_map/convert_element_type | solution.py:122
  93.1 99.8 %all-to-all-done.2 = bf16[8,4,16,2,2880]{4,0,3,2,1:T(8,128)(2,1)} async-done(((bf16[8,4,16,2,2880]{4,0,3,2,1:T(8,128)(2,1)}), bf16[8,4,16,2,2880]{4,0,3,2,1:T(8,128)(2,1)}, u32[]{:S(2)}, u32[]{:S(2)}) %all-to-all-start.2) | async-done | bytes 5898272 | tf_op jit(solution)/shard_map/all_to_all | solution.py:125
  192.9 5.5 all-to-all-start.4
  198.4 13.3 %fusion.6 = f32[16,8,4,2,256]{4,1,3,2,0:T(8,128)S(1)} fusion(bf16[16,2880,256]{2,1,0:T(8,128)(2,1)} %param.20, bf16[8,4,16,2,2880]{4,0,3,2,1:T(8,128)(2,1)} %all-to-all-done.2), kind=kOutput, calls=%fused_computation.9 | convolution fusion | flops 1509949440 | bytes 30539776 | tf_op jit(solution)/shard_map/pkxmd,xdf->pkxmf/dot_general | solution.py:88
  211.7 13.3 %fusion.77 = bf16[8,4,16,2,256]{4,0,3,1,2:T(8,128)(2,1)S(1)} fusion(f32[16,8,4,2,256]{4,1,3,2,0:T(8,128)S(1)} %fusion.6, bf16[16,2880,256]{2,1,0:T(8,128)(2,1)} %param.21, bf16[8,4,16,2,2880]{4,0,3,2,1:T(8,128)(2,1)} %all-to-all-done.2), kind=kOutput, calls=%fused_computation.52 | convolution fusion | flops 1512046592 | bytes 31064064 | tf_op jit(solution)/shard_map/pkxmd,xdf->pkxmf/dot_general | solution.py:91
  225.0 12.9 %convert_bitcast_fusion.1 = bf16[8,4,16,2,2880]{4,0,3,1,2:T(8,128)(2,1)} fusion(bf16[8,4,16,2,256]{4,0,3,1,2:T(8,128)(2,1)S(1)} %fusion.77, bf16[16,256,2880]{1,2,0:T(8,128)(2,1)} %param.22), kind=kOutput, calls=%fused_computation.20 | convolution fusion | flops 1512898560 | bytes 30015488 | tf_op jit(solution)/shard_map/pkxmf,xfd->pkxmd/dot_general | solution.py:95
  237.8 5.7 copy.101
  243.6 87.4 %all-to-all-done.4 = bf16[8,4,16,2,2880]{4,0,3,2,1:T(8,128)(2,1)} async-done(((bf16[8,4,16,2,2880]{4,0,3,2,1:T(8,128)(2,1)}), bf16[8,4,16,2,2880]{4,0,3,2,1:T(8,128)(2,1)}, u32[]{:S(2)}, u32[]{:S(2)}) %all-to-all-start.4) | async-done | bytes 5898272 | tf_op jit(solution)/shard_map/all_to_all | solution.py:125
  331.0 5.8 all-to-all-start.3
  336.8 13.3 %fusion.4 = f32[16,8,4,2,256]{4,1,3,2,0:T(8,128)S(1)} fusion(bf16[16,2880,256]{2,1,0:T(8,128)(2,1)} %param.20, bf16[8,4,16,2,2880]{4,0,3,2,1:T(8,128)(2,1)} %all-to-all-done.4), kind=kOutput, calls=%fused_computation.7 | convolution fusion | flops 1509949440 | bytes 30539776 | tf_op jit(solution)/shard_map/pkxmd,xdf->pkxmf/dot_general | solution.py:88
  350.1 13.3 %fusion.82 = bf16[8,4,16,2,256]{4,0,3,1,2:T(8,128)(2,1)S(1)} fusion(f32[16,8,4,2,256]{4,1,3,2,0:T(8,128)S(1)} %fusion.4, bf16[16,2880,256]{2,1,0:T(8,128)(2,1)} %param.21, bf16[8,4,16,2,2880]{4,0,3,2,1:T(8,128)(2,1)} %all-to-all-done.4), kind=kOutput, calls=%fused_computation.53 | convolution fusion | flops 1512046592 | bytes 31064064 | tf_op jit(solution)/shard_map/pkxmd,xdf->pkxmf/dot_general | solution.py:91
  363.3 12.9 %convert_bitcast_fusion = bf16[8,4,16,2,2880]{4,0,3,1,2:T(8,128)(2,1)} fusion(bf16[8,4,16,2,256]{4,0,3,1,2:T(8,128)(2,1)S(1)} %fusion.82, bf16[16,256,2880]{1,2,0:T(8,128)(2,1)} %param.22), kind=kOutput, calls=%fused_computation.19 | convolution fusion | flops 1512898560 | bytes 30015488 | tf_op jit(solution)/shard_map/pkxmf,xfd->pkxmd/dot_general | solution.py:95
  376.2 5.7 copy.109
  381.9 86.9 %all-to-all-done.3 = bf16[8,4,16,2,2880]{4,0,3,2,1:T(8,128)(2,1)} async-done(((bf16[8,4,16,2,2880]{4,0,3,2,1:T(8,128)(2,1)}), bf16[8,4,16,2,2880]{4,0,3,2,1:T(8,128)(2,1)}, u32[]{:S(2)}, u32[]{:S(2)}) %all-to-all-start.3) | async-done | bytes 5898272 | tf_op jit(solution)/shard_map/all_to_all | solution.py:130
  468.8 5.2 all-to-all-start.5
  474.9 8.7 %all-gather.2 = bf16[8,16,4]{1,2,0:T(4,128)(2,1)S(1)} all-gather(bf16[1,16,4]{1,2,0:T(4,128)(2,1)S(1)} %fusion.134), channel_id=2, replica_groups=mesh['dp'=8,'expert'=4] {'dp'}, dimensions={0}, use_global_device_ids=true | all-gather | bytes 1152 | tf_op jit(solution)/shard_map/all_gather | solution.py:117
  483.9 5.5 fusion.14
  489.5 9.0 %all-gather.3 = bf16[8,16,4]{1,2,0:T(4,128)(2,1)S(1)} all-gather(bf16[1,16,4]{1,2,0:T(4,128)(2,1)S(1)} %fusion.135), channel_id=3, replica_groups=mesh['dp'=8,'expert'=4] {'dp'}, dimensions={0}, use_global_device_ids=true | all-gather | bytes 1152 | tf_op jit(solution)/shard_map/all_gather | solution.py:117
  500.2 1.6 gather_fusion
  502.1 3.1 fusion.138
  505.2 2.5 gather_fusion.1
  507.6 2.5 gather_fusion.2
  510.1 95.9 %all-to-all-done.5 = bf16[8,4,16,2,2880]{4,0,3,2,1:T(8,128)(2,1)} async-done(((bf16[8,4,16,2,2880]{4,0,3,2,1:T(8,128)(2,1)}), bf16[8,4,16,2,2880]{4,0,3,2,1:T(8,128)(2,1)}, u32[]{:S(2)}, u32[]{:S(2)}) %all-to-all-start.5) | async-done | bytes 5898272 | tf_op jit(solution)/shard_map/all_to_all | solution.py:130
  606.0 5.5 fusion.12
  611.6 4.1 broadcast_select_fusion
  615.7 7.7 %reshape.331 = bf16[16,160,8,64]{3,2,1,0:T(8,128)(2,1)} reshape(bf16[160,16,512]{2,1,0:T(8,128)(2,1)} %get-tuple-element.17) | data formatting | bytes 5242880 | tf_op jit(solution)/shard_map/reshape | solution.py:29
  623.4 4.8 reshape.329
  628.2 5.7 bitcast_reduce_fusion
  634.5 1.0 fusion.29
  635.6 1.5 fusion.31
  637.9 1.2 convert_element_type.141
  639.1 9.8 %reduce-scatter.5.cloned.1.call-done = f32[1,16,2880]{2,1,0:T(8,128)} async-done(((f32[8,16,2880]{2,1,0:T(8,128)}), f32[1,16,2880]{2,1,0:T(8,128)}) %reduce-scatter.5.cloned.1.call-update) | async-done | bytes 184336 | tf_op jit(solution)/shard_map/reduce_scatter | solution.py:133
  648.8 1.0 fusion.110
  (84 shorter events, 5.8 us)
Async XLA Ops:
  7.2 467.0 %copy-start = (bf16[2880,64]{0,1:T(8,128)(2,1)S(1)}, bf16[2880,64]{0,1:T(8,128)(2,1)}, u32[]{:S(2)}) copy-start(bf16[2880,64]{0,1:T(8,128)(2,1)} %param.18) | copy-start | bytes 1105924
  7.2 30.6 %all-to-all-start = ((bf16[8,4,16,512]{3,2,1,0:T(8,128)(2,1)}), bf16[8,4,16,512]{3,2,1,0:T(8,128)(2,1)S(1)}, u32[]{:S(2)}, u32[]{:S(2)}) async-start(bf16[8,4,16,512]{3,2,1,0:T(8,128)(2,1)} %param.27), calls=%async_computation | async-start | bytes 1048576 | tf_op jit(solution)/shard_map/all_to_all | solution.py:155
  37.8 16.4 %all-to-all-start.1 = ((bf16[8,4,16,512]{3,2,1,0:T(8,128)(2,1)}), bf16[8,4,16,512]{3,2,1,0:T(8,128)(2,1)S(1)}, u32[]{:S(2)}, u32[]{:S(2)}) async-start(bf16[8,4,16,512]{3,2,1,0:T(8,128)(2,1)} %param.26), calls=%async_computation.1 | async-start | bytes 1048576 | tf_op jit(solution)/shard_map/all_to_all | solution.py:154
  54.3 138.6 %all-to-all-start.2 = ((bf16[8,4,16,2,2880]{4,0,3,2,1:T(8,128)(2,1)}), bf16[8,4,16,2,2880]{4,0,3,2,1:T(8,128)(2,1)}, u32[]{:S(2)}, u32[]{:S(2)}) async-start(bf16[8,4,16,2,2880]{4,0,3,2,1:T(8,128)(2,1)} %bitcast.145), calls=%async_computation.2 | async-start | bytes 12058624 | tf_op jit(solution)/shard_map/all_to_all | solution.py:125
  192.9 138.1 %all-to-all-start.4 = ((bf16[8,4,16,2,2880]{4,0,3,2,1:T(8,128)(2,1)}), bf16[8,4,16,2,2880]{4,0,3,2,1:T(8,128)(2,1)}, u32[]{:S(2)}, u32[]{:S(2)}) async-start(bf16[8,4,16,2,2880]{4,0,3,2,1:T(8,128)(2,1)} %bitcast.146), calls=%async_computation.5 | async-start | bytes 12058624 | tf_op jit(solution)/shard_map/all_to_all | solution.py:125
  331.0 137.8 %all-to-all-start.3 = ((bf16[8,4,16,2,2880]{4,0,3,2,1:T(8,128)(2,1)}), bf16[8,4,16,2,2880]{4,0,3,2,1:T(8,128)(2,1)}, u32[]{:S(2)}, u32[]{:S(2)}) async-start(bf16[8,4,16,2,2880]{4,0,3,2,1:T(8,128)(2,1)} %copy.101), calls=%async_computation.3 | async-start | bytes 12058624 | tf_op jit(solution)/shard_map/all_to_all | solution.py:130
  381.9 92.2 %copy-start.5 = (bf16[2,16,2880]{2,1,0:T(8,128)(2,1)S(1)}, bf16[2,16,2880]{2,1,0:T(8,128)(2,1)}, u32[]{:S(2)}) copy-start(bf16[2,16,2880]{2,1,0:T(8,128)(2,1)} %param.16) | copy-start | bytes 552964
  381.9 92.2 %copy-start.9 = (f32[2880]{0:T(1024)S(1)}, f32[2880]{0:T(1024)}, u32[]{:S(2)}) copy-start(f32[2880]{0:T(1024)} %param.17) | copy-start | bytes 34564
  468.8 137.2 %all-to-all-start.5 = ((bf16[8,4,16,2,2880]{4,0,3,2,1:T(8,128)(2,1)}), bf16[8,4,16,2,2880]{4,0,3,2,1:T(8,128)(2,1)}, u32[]{:S(2)}, u32[]{:S(2)}) async-start(bf16[8,4,16,2,2880]{4,0,3,2,1:T(8,128)(2,1)} %copy.109), calls=%async_computation.6 | async-start | bytes 12058624 | tf_op jit(solution)/shard_map/all_to_all | solution.py:130
  474.0 24.5 %copy-start.12 = (s32[1,16]{1,0:T(1,128)S(1)}, s32[1,16]{1,0:T(1,128)}, u32[]{:S(2)}) copy-start(s32[1,16]{1,0:T(1,128)} %param.28) | copy-start | bytes 196
  474.0 25.3 %copy-start.7 = (bf16[2,16,4096]{2,1,0:T(8,128)(2,1)S(1)}, bf16[2,16,4096]{2,1,0:T(8,128)(2,1)}, u32[]{:S(2)}) copy-start(bf16[2,16,4096]{2,1,0:T(8,128)(2,1)} %param.23) | copy-start | bytes 786436
  474.0 25.9 %copy-start.10 = (bf16[2,16,512]{2,1,0:T(8,128)(2,1)S(1)}, bf16[2,16,512]{2,1,0:T(8,128)(2,1)}, u32[]{:S(2)}) copy-start(bf16[2,16,512]{2,1,0:T(8,128)(2,1)} %param.24) | copy-start | bytes 98308
  474.1 26.0 %copy-start.11 = (bf16[2,16,512]{2,1,0:T(8,128)(2,1)S(1)}, bf16[2,16,512]{2,1,0:T(8,128)(2,1)}, u32[]{:S(2)}) copy-start(bf16[2,16,512]{2,1,0:T(8,128)(2,1)} %param.25) | copy-start | bytes 98308
  474.1 26.1 %copy-start.1 = (s32[1,32]{1,0:T(1,128)S(1)}, s32[1,32]{1,0:T(1,128)}, u32[]{:S(2)}) copy-start(s32[1,32]{1,0:T(1,128)} %param.29) | copy-start | bytes 388
  474.1 165.0 %reduce-scatter.3.cloned.1.call-start = ((), (), s32[]{:S(2)}) async-start(), calls=%async_computation.8 | async-start | bytes 1695744 | tf_op jit(solution)/shard_map/reduce_scatter | solution.py:133
  489.4 159.4 %reduce-scatter.5.cloned.1.call-start = ((), (), s32[]{:S(2)}) async-start(), calls=%async_computation.9 | async-start | bytes 1695744 | tf_op jit(solution)/shard_map/reduce_scatter | solution.py:133
  499.9 7.7 %copy-start.6 = (bf16[2,16,8,8,64]{4,3,2,1,0:T(8,128)(2,1)}, bf16[2,16,8,8,64]{4,3,2,1,0:T(8,128)(2,1)S(1)}, u32[]{:S(2)}) copy-start(bf16[2,16,8,8,64]{4,3,2,1,0:T(8,128)(2,1)S(1)} %reshape.332) | copy-start | bytes 786436
  510.1 101.4 %copy-start.2 = (bf16[160,16,512]{2,1,0:T(8,128)(2,1)S(1)}, bf16[160,16,512]{2,1,0:T(8,128)(2,1)}, u32[]{:S(2)}) copy-start(bf16[160,16,512]{2,1,0:T(8,128)(2,1)} %gather_fusion.1) | copy-start | bytes 7864324
  615.7 7.7 %copy-start.3 = (bf16[160,16,512]{2,1,0:T(8,128)(2,1)S(1)}, bf16[160,16,512]{2,1,0:T(8,128)(2,1)}, u32[]{:S(2)}) copy-start(bf16[160,16,512]{2,1,0:T(8,128)(2,1)} %get-tuple-element.18) | copy-start | bytes 7864324
  628.2 5.8 copy-start.8
  628.2 7.4 %copy-start.4 = (bf16[16,160,8,64]{3,2,1,0:T(8,128)(2,1)S(1)}, bf16[16,160,8,64]{3,2,1,0:T(8,128)(2,1)}, u32[]{:S(2)}) copy-start(bf16[16,160,8,64]{3,2,1,0:T(8,128)(2,1)} %reshape.329) | copy-start | bytes 7864324
Sparse Core Ops, SparseCore 0:
  489.5 38.6 reduce-scatter.2
  611.7 37.1 reduce-scatter.4
where the time goes:
time: 665 us; the launch traced here: 658 us
  waiting for transfers between devices  380 us (57%)
  matrix products  109 us (16%)
  blocking collectives  58.9 us (9%)
  local copies, waits for them, and re-layouts  50.8 us (8%)
  starting transfers between devices  30.6 us (5%)
  between operations  14.8 us (2%)
  other arithmetic  13.5 us (2%)
    all_to_all x2, waiting for transfers between devices, moe_step(): lax.all_to_all(packed, 'expert', split_axis=1, concat_axis=1, tiled=True)  187 us
    all_to_all x2, waiting for transfers between devices, moe_step(): lax.all_to_all(partial_out, 'expert', split_axis=1, concat_axis=1, tiled=...  183 us
    dot_general x2, matrix products, expert_block(): jnp.einsum('pkxmd,xdf->pkxmf', slot_rows, w_gate, preferred_element_type=...  26.6 us
    dot_general x2, matrix products, expert_block(): jnp.einsum('pkxmd,xdf->pkxmf', slot_rows, w_up, preferred_element_type=jn...  26.5 us
    dot_general x2, matrix products, expert_block(): jnp.einsum('pkxmf,xfd->pkxmd', hidden_act, w_down, preferred_element_type...  25.7 us
    all_gather x2, blocking collectives, moe_step(): lax.all_gather(expert_ids.astype(jnp.bfloat16)[None], 'dp', axis=0, tiled...  21.4 us
    all_gather x2, blocking collectives, moe_step(): lax.all_gather(normed[None], 'dp', axis=0, tiled=True)  19.7 us
    all_gather x2, blocking collectives, moe_step(): lax.all_gather(gate_vals[None], 'dp', axis=0, tiled=True)  17.7 us
  transfers between devices with their start and end apart: 8, of which 5 were waited for; matrix products, arithmetic and copies ran while one was open for 26% of the time, Pallas kernels for 0%

commit v1 on v0

--- a/solution.py
+++ b/solution.py
@@ -127,7 +127,12 @@
         w_up,
         w_down,
     )
-    returned = lax.all_to_all(partial_out, "expert", split_axis=1, concat_axis=1, tiled=True)
+    returned = jnp.concatenate(
+        lax.all_to_all(
+            jnp.stack(jnp.split(partial_out, lax.axis_size("expert"), axis=1)), "expert", 0, 0
+        ),
+        axis=1,
+    )
     returned = returned.reshape(returned.shape[0], EXPERTS * MOST, model_width)
     row_terms = jnp.einsum("prs,psd->prd", weights, returned, preferred_element_type=jnp.float32)
     branch_out = lax.psum_scatter(row_terms, "dp", scatter_dimension=0, tiled=True)[0]

time: 665 us -> 664 us (level)
  other arithmetic: 13.5 us -> 22 us
    convert_element_type x2 -> x0, local copies, waits for them, and re-layouts: 11.4 us -> none  [expert_block(): return jnp.einsum('pkxmf,xfd->pkxmd', hidden_act, w_down, preferred_eleme...]
    another operation x2 -> x4, other arithmetic: 0.16 us -> 8.59 us  [the longest x2 8.44 us: moe_step(): jnp.stack(jnp.split(partial_out, lax.axis_size('expert'), axis=1))]
  transfers between devices with their start and end apart: 8 -> 8, of which waited for: 5 -> 5; matrix products, arithmetic and copies ran while one was open for 26% -> 27% of each run, Pallas kernels for 0% -> 0%
where the time goes in v1:
time: 664 us; the launch traced here: 658 us
  waiting for transfers between devices  376 us (57%)
  matrix products  109 us (16%)
  blocking collectives  58.9 us (9%)
  local copies, waits for them, and re-layouts  45.8 us (7%)
  starting transfers between devices  30.5 us (5%)
  other arithmetic  22 us (3%)
  between operations  14.8 us (2%)
    all_to_all x2, waiting for transfers between devices, moe_step(): lax.all_to_all(packed, 'expert', split_axis=1, concat_axis=1, tiled=True)  186 us
    all_to_all x2, waiting for transfers between devices, moe_step(): lax.all_to_all(jnp.stack(jnp.split(partial_out, lax.axis_size('expert'),...  181 us
    dot_general x2, matrix products, expert_block(): jnp.einsum('pkxmd,xdf->pkxmf', slot_rows, w_gate, preferred_element_type=...  26.6 us
    dot_general x2, matrix products, expert_block(): jnp.einsum('pkxmd,xdf->pkxmf', slot_rows, w_up, preferred_element_type=jn...  26.5 us
    dot_general x2, matrix products, expert_block(): jnp.einsum('pkxmf,xfd->pkxmd', hidden_act, w_down, preferred_element_type...  25.8 us
    all_gather x2, blocking collectives, moe_step(): lax.all_gather(expert_ids.astype(jnp.bfloat16)[None], 'dp', axis=0, tiled...  21.4 us
    all_gather x2, blocking collectives, moe_step(): lax.all_gather(normed[None], 'dp', axis=0, tiled=True)  19.7 us
    all_gather x2, blocking collectives, moe_step(): lax.all_gather(gate_vals[None], 'dp', axis=0, tiled=True)  17.8 us
  transfers between devices with their start and end apart: 8, of which 5 were waited for; matrix products, arithmetic and copies ran while one was open for 27% of the time, Pallas kernels for 0%

profile of v1, /device:TPU:0, one launch (start us, length us, event | category | flops | bytes accessed | tf_op | source)
XLA Modules:
  0.0 657.6 jit_solution(6123735257518678812)
XLA Ops:
  7.2 5.3 all-to-all-start
  13.2 12.1 %all_gather.21 = bf16[8,16,4]{1,2,0:T(4,128)(2,1)S(1)} all-gather(bf16[1,16,4]{1,2,0:T(4,128)(2,1)S(1)} %get-tuple-element.21), channel_id=1, replica_groups=mesh['dp'=8,'expert'=4] {'dp'}, dimensions={0}, use_global_device_ids=true | all-gather | bytes 1152 | tf_op jit(solution)/shard_map/all_gather | solution.py:116
  25.5 1.1 fusion.105
  26.6 1.1 fusion.109
  28.4 9.4 %all_gather.23 = bf16[8,16,2880]{2,1,0:T(8,128)(2,1)S(1)} all-gather(bf16[1,16,2880]{2,1,0:T(8,128)(2,1)S(1)} %get-tuple-element.16), channel_id=1, replica_groups=mesh['dp'=8,'expert'=4] {'dp'}, dimensions={0}, use_global_device_ids=true | all-gather | bytes 829440 | tf_op jit(solution)/shard_map/all_gather | solution.py:115
  37.8 3.5 all-to-all-start.1
  41.5 4.0 convolution_convert_fusion
  45.5 8.8 %copy.124 = bf16[8,128,2880]{2,0,1:T(8,128)(2,1)} copy(bf16[8,128,2880]{1,2,0:T(8,128)(2,1)} %convolution_convert_fusion) | data formatting | bytes 11796480 | tf_op jit(solution)/shard_map/convert_element_type | solution.py:122
  54.3 5.3 all-to-all-start.4
  59.5 9.3 %all_gather.18 = bf16[8,16,4]{1,2,0:T(4,128)(2,1)S(1)} all-gather(bf16[1,16,4]{1,2,0:T(4,128)(2,1)S(1)} %get-tuple-element.22), channel_id=1, replica_groups=mesh['dp'=8,'expert'=4] {'dp'}, dimensions={0}, use_global_device_ids=true | all-gather | bytes 1152 | tf_op jit(solution)/shard_map/all_gather | solution.py:116
  69.1 0.7 select_reduce_fusion.3
  70.0 10.4 %all_gather.20 = bf16[8,16,2880]{2,1,0:T(8,128)(2,1)S(1)} all-gather(bf16[1,16,2880]{2,1,0:T(8,128)(2,1)S(1)} %get-tuple-element.15), channel_id=1, replica_groups=mesh['dp'=8,'expert'=4] {'dp'}, dimensions={0}, use_global_device_ids=true | all-gather | bytes 829440 | tf_op jit(solution)/shard_map/all_gather | solution.py:115
  80.3 4.0 convolution_convert_fusion.1
  84.3 8.8 %copy.114 = bf16[8,128,2880]{2,0,1:T(8,128)(2,1)} copy(bf16[8,128,2880]{1,2,0:T(8,128)(2,1)} %convolution_convert_fusion.1) | data formatting | bytes 11796480 | tf_op jit(solution)/shard_map/convert_element_type | solution.py:122
  93.1 99.8 %all-to-all-done.4 = bf16[8,4,16,2,2880]{4,0,3,2,1:T(8,128)(2,1)} async-done(((bf16[8,4,16,2,2880]{4,0,3,2,1:T(8,128)(2,1)}), bf16[8,4,16,2,2880]{4,0,3,2,1:T(8,128)(2,1)}, u32[]{:S(2)}, u32[]{:S(2)}) %all-to-all-start.4) | async-done | bytes 5898272 | tf_op jit(solution)/shard_map/all_to_all | solution.py:125
  192.9 5.7 all-to-all-start.2
  198.7 13.3 %fusion.4 = f32[16,8,4,2,256]{4,1,3,2,0:T(8,128)S(1)} fusion(bf16[16,2880,256]{2,1,0:T(8,128)(2,1)} %param.20, bf16[8,4,16,2,2880]{4,0,3,2,1:T(8,128)(2,1)} %all-to-all-done.4), kind=kOutput, calls=%fused_computation.7 | convolution fusion | flops 1509949440 | bytes 30539776 | tf_op jit(solution)/shard_map/pkxmd,xdf->pkxmf/dot_general | solution.py:88
  212.0 13.3 %fusion.82 = bf16[8,4,16,2,256]{4,0,3,1,2:T(8,128)(2,1)S(1)} fusion(f32[16,8,4,2,256]{4,1,3,2,0:T(8,128)S(1)} %fusion.4, bf16[16,2880,256]{2,1,0:T(8,128)(2,1)} %param.21, bf16[8,4,16,2,2880]{4,0,3,2,1:T(8,128)(2,1)} %all-to-all-done.4), kind=kOutput, calls=%fused_computation.63 | convolution fusion | flops 1512046592 | bytes 31064064 | tf_op jit(solution)/shard_map/pkxmd,xdf->pkxmf/dot_general | solution.py:91
  225.2 12.9 %convert_bitcast_fusion = bf16[8,4,16,2,2880]{4,0,3,1,2:T(8,128)(2,1)} fusion(bf16[8,4,16,2,256]{4,0,3,1,2:T(8,128)(2,1)S(1)} %fusion.82, bf16[16,256,2880]{1,2,0:T(8,128)(2,1)} %param.22), kind=kOutput, calls=%fused_computation.21 | convolution fusion | flops 1512898560 | bytes 30015488 | tf_op jit(solution)/shard_map/pkxmf,xfd->pkxmd/dot_general | solution.py:95
  238.1 3.2 slice_bitcast_fusion.3
  241.3 4.2 pad_maximum_fusion.1
  245.4 85.8 %all-to-all-done.2 = bf16[8,4,16,2,2880]{4,0,3,2,1:T(8,128)(2,1)} async-done(((bf16[8,4,16,2,2880]{4,0,3,2,1:T(8,128)(2,1)}), bf16[8,4,16,2,2880]{4,0,3,2,1:T(8,128)(2,1)}, u32[]{:S(2)}, u32[]{:S(2)}) %all-to-all-start.2) | async-done | bytes 5898272 | tf_op jit(solution)/shard_map/all_to_all | solution.py:125
  331.3 5.4 all-to-all-start.5
  336.7 13.3 %fusion.6 = f32[16,8,4,2,256]{4,1,3,2,0:T(8,128)S(1)} fusion(bf16[16,2880,256]{2,1,0:T(8,128)(2,1)} %param.20, bf16[8,4,16,2,2880]{4,0,3,2,1:T(8,128)(2,1)} %all-to-all-done.2), kind=kOutput, calls=%fused_computation.9 | convolution fusion | flops 1509949440 | bytes 30539776 | tf_op jit(solution)/shard_map/pkxmd,xdf->pkxmf/dot_general | solution.py:88
  350.0 13.3 %fusion.77 = bf16[8,4,16,2,256]{4,0,3,1,2:T(8,128)(2,1)S(1)} fusion(f32[16,8,4,2,256]{4,1,3,2,0:T(8,128)S(1)} %fusion.6, bf16[16,2880,256]{2,1,0:T(8,128)(2,1)} %param.21, bf16[8,4,16,2,2880]{4,0,3,2,1:T(8,128)(2,1)} %all-to-all-done.2), kind=kOutput, calls=%fused_computation.62 | convolution fusion | flops 1512046592 | bytes 31064064 | tf_op jit(solution)/shard_map/pkxmd,xdf->pkxmf/dot_general | solution.py:91
  363.3 12.9 %convert_bitcast_fusion.1 = bf16[8,4,16,2,2880]{4,0,3,1,2:T(8,128)(2,1)} fusion(bf16[8,4,16,2,256]{4,0,3,1,2:T(8,128)(2,1)S(1)} %fusion.77, bf16[16,256,2880]{1,2,0:T(8,128)(2,1)} %param.22), kind=kOutput, calls=%fused_computation.22 | convolution fusion | flops 1512898560 | bytes 30015488 | tf_op jit(solution)/shard_map/pkxmf,xfd->pkxmd/dot_general | solution.py:95
  376.2 3.2 slice_bitcast_fusion.7
  379.4 4.3 pad_maximum_fusion
  383.6 85.1 %all-to-all-done.5 = bf16[4,8,1,16,2,2880]{5,1,4,3,2,0:T(8,128)(2,1)} async-done(((bf16[4,8,1,16,2,2880]{5,1,4,3,2,0:T(8,128)(2,1)}), bf16[4,8,1,16,2,2880]{5,1,4,3,2,0:T(8,128)(2,1)}, u32[]{:S(2)}, u32[]{:S(2)}) %all-to-all-start.5) | async-done | bytes 5898272 | tf_op jit(solution)/shard_map/all_to_all | solution.py:131
  468.7 5.2 all-to-all-start.3
  474.8 8.9 %all-gather.3 = bf16[8,16,4]{1,2,0:T(4,128)(2,1)S(1)} all-gather(bf16[1,16,4]{1,2,0:T(4,128)(2,1)S(1)} %fusion.135), channel_id=3, replica_groups=mesh['dp'=8,'expert'=4] {'dp'}, dimensions={0}, use_global_device_ids=true | all-gather | bytes 1152 | tf_op jit(solution)/shard_map/all_gather | solution.py:117
  484.0 5.5 fusion.12
  489.6 8.9 %all-gather.2 = bf16[8,16,4]{1,2,0:T(4,128)(2,1)S(1)} all-gather(bf16[1,16,4]{1,2,0:T(4,128)(2,1)S(1)} %fusion.134), channel_id=2, replica_groups=mesh['dp'=8,'expert'=4] {'dp'}, dimensions={0}, use_global_device_ids=true | all-gather | bytes 1152 | tf_op jit(solution)/shard_map/all_gather | solution.py:117
  500.1 1.6 gather_fusion
  502.0 3.1 fusion.138
  505.1 2.5 gather_fusion.1
  507.6 2.5 gather_fusion.2
  510.1 95.9 %all-to-all-done.3 = bf16[4,8,1,16,2,2880]{5,1,4,3,2,0:T(8,128)(2,1)} async-done(((bf16[4,8,1,16,2,2880]{5,1,4,3,2,0:T(8,128)(2,1)}), bf16[4,8,1,16,2,2880]{5,1,4,3,2,0:T(8,128)(2,1)}, u32[]{:S(2)}, u32[]{:S(2)}) %all-to-all-start.3) | async-done | bytes 5898272 | tf_op jit(solution)/shard_map/all_to_all | solution.py:131
  606.0 5.5 fusion.14
  611.5 4.1 broadcast_select_fusion
  615.6 7.7 %reshape.331 = bf16[16,160,8,64]{3,2,1,0:T(8,128)(2,1)} reshape(bf16[160,16,512]{2,1,0:T(8,128)(2,1)} %get-tuple-element.25) | data formatting | bytes 5242880 | tf_op jit(solution)/shard_map/reshape | solution.py:29
  623.3 4.8 reshape.329
  628.2 5.7 bitcast_reduce_fusion
  634.5 1.0 fusion.29
  635.6 1.5 fusion.31
  637.9 1.2 convert_element_type.141
  639.1 9.7 %reduce-scatter.3.cloned.1.call-done = f32[1,16,2880]{2,1,0:T(8,128)} async-done(((f32[8,16,2880]{2,1,0:T(8,128)}), f32[1,16,2880]{2,1,0:T(8,128)}) %reduce-scatter.3.cloned.1.call-update) | async-done | bytes 184336 | tf_op jit(solution)/shard_map/reduce_scatter | solution.py:138
  648.7 1.0 fusion.110
  (86 shorter events, 7.3 us)
Async XLA Ops:
  7.2 466.9 %copy-start = (bf16[2880,64]{0,1:T(8,128)(2,1)S(1)}, bf16[2880,64]{0,1:T(8,128)(2,1)}, u32[]{:S(2)}) copy-start(bf16[2880,64]{0,1:T(8,128)(2,1)} %param.18) | copy-start | bytes 1105924
  7.2 30.6 %all-to-all-start = ((bf16[8,4,16,512]{3,2,1,0:T(8,128)(2,1)}), bf16[8,4,16,512]{3,2,1,0:T(8,128)(2,1)S(1)}, u32[]{:S(2)}, u32[]{:S(2)}) async-start(bf16[8,4,16,512]{3,2,1,0:T(8,128)(2,1)} %param.27), calls=%async_computation | async-start | bytes 1048576 | tf_op jit(solution)/shard_map/all_to_all | solution.py:160
  37.8 16.4 %all-to-all-start.1 = ((bf16[8,4,16,512]{3,2,1,0:T(8,128)(2,1)}), bf16[8,4,16,512]{3,2,1,0:T(8,128)(2,1)S(1)}, u32[]{:S(2)}, u32[]{:S(2)}) async-start(bf16[8,4,16,512]{3,2,1,0:T(8,128)(2,1)} %param.26), calls=%async_computation.1 | async-start | bytes 1048576 | tf_op jit(solution)/shard_map/all_to_all | solution.py:159
  54.3 138.7 %all-to-all-start.4 = ((bf16[8,4,16,2,2880]{4,0,3,2,1:T(8,128)(2,1)}), bf16[8,4,16,2,2880]{4,0,3,2,1:T(8,128)(2,1)}, u32[]{:S(2)}, u32[]{:S(2)}) async-start(bf16[8,4,16,2,2880]{4,0,3,2,1:T(8,128)(2,1)} %bitcast.177), calls=%async_computation.5 | async-start | bytes 12058624 | tf_op jit(solution)/shard_map/all_to_all | solution.py:125
  192.9 138.3 %all-to-all-start.2 = ((bf16[8,4,16,2,2880]{4,0,3,2,1:T(8,128)(2,1)}), bf16[8,4,16,2,2880]{4,0,3,2,1:T(8,128)(2,1)}, u32[]{:S(2)}, u32[]{:S(2)}) async-start(bf16[8,4,16,2,2880]{4,0,3,2,1:T(8,128)(2,1)} %bitcast.178), calls=%async_computation.2 | async-start | bytes 12058624 | tf_op jit(solution)/shard_map/all_to_all | solution.py:125
  331.3 137.5 %all-to-all-start.5 = ((bf16[4,8,1,16,2,2880]{5,1,4,3,2,0:T(8,128)(2,1)}), bf16[4,8,1,16,2,2880]{5,1,4,3,2,0:T(8,128)(2,1)}, u32[]{:S(2)}, u32[]{:S(2)}) async-start(bf16[4,8,1,16,2,2880]{5,1,4,3,2,0:T(8,128)(2,1)} %pad_maximum_fusion.1), calls=%async_computation.6 | async-start | bytes 12058624 | tf_op jit(solution)/shard_map/all_to_all | solution.py:131
  383.6 90.4 %copy-start.5 = (bf16[2,16,2880]{2,1,0:T(8,128)(2,1)S(1)}, bf16[2,16,2880]{2,1,0:T(8,128)(2,1)}, u32[]{:S(2)}) copy-start(bf16[2,16,2880]{2,1,0:T(8,128)(2,1)} %param.16) | copy-start | bytes 552964
  383.6 90.4 %copy-start.9 = (f32[2880]{0:T(1024)S(1)}, f32[2880]{0:T(1024)}, u32[]{:S(2)}) copy-start(f32[2880]{0:T(1024)} %param.17) | copy-start | bytes 34564
  468.7 137.2 %all-to-all-start.3 = ((bf16[4,8,1,16,2,2880]{5,1,4,3,2,0:T(8,128)(2,1)}), bf16[4,8,1,16,2,2880]{5,1,4,3,2,0:T(8,128)(2,1)}, u32[]{:S(2)}, u32[]{:S(2)}) async-start(bf16[4,8,1,16,2,2880]{5,1,4,3,2,0:T(8,128)(2,1)} %pad_maximum_fusion), calls=%async_computation.3 | async-start | bytes 12058624 | tf_op jit(solution)/shard_map/all_to_all | solution.py:131
  474.0 24.5 %copy-start.12 = (s32[1,16]{1,0:T(1,128)S(1)}, s32[1,16]{1,0:T(1,128)}, u32[]{:S(2)}) copy-start(s32[1,16]{1,0:T(1,128)} %param.28) | copy-start | bytes 196
  474.0 25.3 %copy-start.7 = (bf16[2,16,4096]{2,1,0:T(8,128)(2,1)S(1)}, bf16[2,16,4096]{2,1,0:T(8,128)(2,1)}, u32[]{:S(2)}) copy-start(bf16[2,16,4096]{2,1,0:T(8,128)(2,1)} %param.23) | copy-start | bytes 786436
  474.0 165.1 %reduce-scatter.5.cloned.1.call-start = ((), (), s32[]{:S(2)}) async-start(), calls=%async_computation.9 | async-start | bytes 1695744 | tf_op jit(solution)/shard_map/reduce_scatter | solution.py:138
  474.3 25.6 %copy-start.10 = (bf16[2,16,512]{2,1,0:T(8,128)(2,1)S(1)}, bf16[2,16,512]{2,1,0:T(8,128)(2,1)}, u32[]{:S(2)}) copy-start(bf16[2,16,512]{2,1,0:T(8,128)(2,1)} %param.24) | copy-start | bytes 98308
  474.3 25.7 %copy-start.11 = (bf16[2,16,512]{2,1,0:T(8,128)(2,1)S(1)}, bf16[2,16,512]{2,1,0:T(8,128)(2,1)}, u32[]{:S(2)}) copy-start(bf16[2,16,512]{2,1,0:T(8,128)(2,1)} %param.25) | copy-start | bytes 98308
  474.3 25.8 %copy-start.1 = (s32[1,32]{1,0:T(1,128)S(1)}, s32[1,32]{1,0:T(1,128)}, u32[]{:S(2)}) copy-start(s32[1,32]{1,0:T(1,128)} %param.29) | copy-start | bytes 388
  489.5 159.2 %reduce-scatter.3.cloned.1.call-start = ((), (), s32[]{:S(2)}) async-start(), calls=%async_computation.8 | async-start | bytes 1695744 | tf_op jit(solution)/shard_map/reduce_scatter | solution.py:138
  499.9 7.7 %copy-start.6 = (bf16[2,16,8,8,64]{4,3,2,1,0:T(8,128)(2,1)}, bf16[2,16,8,8,64]{4,3,2,1,0:T(8,128)(2,1)S(1)}, u32[]{:S(2)}) copy-start(bf16[2,16,8,8,64]{4,3,2,1,0:T(8,128)(2,1)S(1)} %reshape.332) | copy-start | bytes 786436
  510.1 101.4 %copy-start.2 = (bf16[160,16,512]{2,1,0:T(8,128)(2,1)S(1)}, bf16[160,16,512]{2,1,0:T(8,128)(2,1)}, u32[]{:S(2)}) copy-start(bf16[160,16,512]{2,1,0:T(8,128)(2,1)} %gather_fusion.1) | copy-start | bytes 7864324
  615.6 7.7 %copy-start.3 = (bf16[160,16,512]{2,1,0:T(8,128)(2,1)S(1)}, bf16[160,16,512]{2,1,0:T(8,128)(2,1)}, u32[]{:S(2)}) copy-start(bf16[160,16,512]{2,1,0:T(8,128)(2,1)} %get-tuple-element.26) | copy-start | bytes 7864324
  628.1 5.8 copy-start.8
  628.1 7.5 %copy-start.4 = (bf16[16,160,8,64]{3,2,1,0:T(8,128)(2,1)S(1)}, bf16[16,160,8,64]{3,2,1,0:T(8,128)(2,1)}, u32[]{:S(2)}) copy-start(bf16[16,160,8,64]{3,2,1,0:T(8,128)(2,1)} %reshape.329) | copy-start | bytes 7864324
Sparse Core Ops, SparseCore 0:
  489.7 38.6 reduce-scatter.4
  611.6 37.0 reduce-scatter.2
